TPU v7x, 32 devices: a whole 2x2x4 slice. The times are simulated.
32 devices in a mesh: fsdp: 16 (over z, x, core), tp: 2 (over y).
Axes of the slice: x: 2, y: 2, z: 4, core: 2. Of those that a mesh axis runs over, the one named last changes fastest.
Arguments:
- xbc: bfloat16 [4096, 8, 2304], P('fsdp', 'tp'), may hold values from -6 to 6
- dt_raw: bfloat16 [256, 4096], P('tp', 'fsdp'), may hold values from -3 to 3
- conv_weight: bfloat16 [4, 8, 2304], P(None, 'tp'), may hold values from -3 to 3
- conv_bias: bfloat16 [8, 2304], P('tp'), may hold values from -3 to 3
- dt_bias: float32 [256], P('tp'), may hold values from -13 to 0
- a_log: float32 [256], P('tp'), may hold values from -1.5 to -0.1
- d_skip: float32 [256], P('tp'), may hold values from 0.5 to 1.5
Outputs:
- mixed: float32 [4096, 16384], P(('fsdp', 'tp'))
All inputs are finite; a program needn't handle non-finite values.
Results may differ from a plain program's by a relative error of at most 0.0016.
Values may be sent and summed in bfloat16 or wider, within the bound.
No kernel may reach another device: no remote copies, remote signals or barrier semaphores. Data moves between devices by JAX's collectives and lax.ppermute only.
A program may use at most 256 MiB of HBM per device.

v0:
```python
import jax
import jax.numpy as jnp
from jax import lax
from jax.sharding import Mesh, PartitionSpec as P

HEAD_DIM = 64
STATE = 128
SEQ = ("fh", "fl")


def convolve(xbc, conv_weight, conv_bias, seq_count):
    row_count = xbc.shape[0]
    tap_count = conv_weight.shape[0]
    rim = xbc[row_count - (tap_count - 1) :]
    rim_rows = lax.ppermute(rim, SEQ, [(d, d + 1) for d in range(seq_count - 1)])
    padded = jnp.concatenate([rim_rows, xbc], axis=0)
    summed = conv_bias.astype(jnp.float32)[None]
    for k in range(tap_count):
        summed = summed + conv_weight[k].astype(jnp.float32)[None] * padded[
            k : k + row_count
        ].astype(jnp.float32)
    return jax.nn.silu(summed).astype(jnp.bfloat16)


def shards(xbc, dt_raw, conv_weight, conv_bias, dt_bias, a_log, d_skip, seq_count, tp_count):
    row_count, group_count, _ = xbc.shape
    head_count = dt_raw.shape[0]
    per_group = head_count // group_count
    inner_width = per_group * HEAD_DIM
    exact = lax.Precision.HIGHEST
    f32 = jnp.float32

    activated = convolve(xbc, conv_weight, conv_bias, seq_count)
    chunk = min(128, row_count)
    nck = row_count // chunk
    values = activated[:, :, :inner_width].reshape(nck, chunk, group_count, per_group, HEAD_DIM)
    b_part = activated[:, :, inner_width : inner_width + STATE].reshape(nck, chunk, group_count, STATE)
    c_part = activated[:, :, inner_width + STATE :].reshape(nck, chunk, group_count, STATE)

    step_sizes = jax.nn.softplus(dt_raw.astype(f32) + dt_bias[:, None])
    log_rates = -jnp.exp(a_log)[:, None] * step_sizes
    steps = step_sizes.reshape(group_count, per_group, nck, chunk)
    rates = log_rates.reshape(group_count, per_group, nck, chunk)
    cum = jnp.cumsum(rates, axis=3)
    chunk_log = cum[..., -1]

    values32 = values
    weights = jnp.exp(chunk_log[..., None] - cum) * steps
    weighted = values32 * jnp.transpose(weights, (2, 3, 0, 1))[..., None]
    chunk_states = jnp.einsum("ksgn,ksgjp->kgjpn", b_part.astype(f32), weighted, precision=exact)

    running = jnp.zeros_like(chunk_states[0])
    local_list = []
    for k in range(nck):
        local_list.append(running)
        running = jnp.exp(chunk_log[:, :, k])[..., None, None] * running + chunk_states[k]
    dev_state = running
    cum_dev = cum + jnp.concatenate(
        [jnp.zeros_like(chunk_log[..., :1]), jnp.cumsum(chunk_log, axis=2)[..., :-1]], axis=2
    )[..., None]
    dev_log = jnp.sum(chunk_log, axis=2)

    def intra(side):
        values32, b_part, c_part, local_list = side
        causal = lax.broadcasted_iota(jnp.int32, (chunk, chunk), 0) >= lax.broadcasted_iota(
            jnp.int32, (chunk, chunk), 1
        )
        scores = jnp.einsum("ktgn,ksgn->kgts", c_part, b_part, preferred_element_type=f32)
        gaps = cum[..., :, None] - cum[..., None, :]
        decays = jnp.exp(jnp.where(causal, gaps, -jnp.inf))
        mixing = decays * jnp.transpose(scores, (1, 0, 2, 3))[:, None] * steps[..., None, :]
        output = jnp.einsum("gjkts,ksgjp->ktgjp", mixing, values32, precision=exact)
        output = output + d_skip.reshape(group_count, per_group)[None, None, :, :, None] * values32

        if nck == 1:
            return output
        later = jnp.stack(local_list[1:], axis=0)
        carried_local = jnp.einsum("ktgn,kgjpn->ktgjp", c_part[1:].astype(f32), later, precision=exact)
        scale = jnp.transpose(jnp.exp(cum[:, :, 1:]), (2, 3, 0, 1))[..., None]
        return jnp.concatenate([output[:1], output[1:] + scale * carried_local], axis=0)

    lo = lax.axis_index("fl")
    pair_count = seq_count // 2
    half = per_group // 2
    swap = [(0, 1), (1, 0)]
    partner_log = lax.ppermute(dev_log, "fl", swap)
    first_log = jnp.where(lo == 0, dev_log, partner_log)
    second_log = jnp.where(lo == 0, partner_log, dev_log)
    own_half = lax.dynamic_slice_in_dim(dev_state, lo * half, half, axis=1)
    other_half = lax.dynamic_slice_in_dim(dev_state, (1 - lo) * half, half, axis=1)
    recv_a = lax.ppermute(other_half, "fl", swap)
    first_state = jnp.where(lo == 0, own_half, recv_a)
    second_state = jnp.where(lo == 0, recv_a, own_half)
    second_log_half = lax.dynamic_slice_in_dim(second_log, lo * half, half, axis=1)
    first_log_half = lax.dynamic_slice_in_dim(first_log, lo * half, half, axis=1)
    pair_state = jnp.exp(second_log_half)[..., None, None] * first_state + second_state
    pair_log_half = first_log_half + second_log_half
    first_size = half - half // 4
    sizes = (first_size, half - first_size)
    starts = (0, first_size)
    c32 = c_part.astype(f32)
    first_decay = jnp.exp(first_log_half)[..., None, None]
    grow = jnp.exp(cum_dev).reshape(group_count, 2, half, nck, chunk)
    by_chunk = nck == tp_count

    def finish(pair_in, q, intra_out):
        part = slice(starts[q], starts[q] + sizes[q])
        own_in = jnp.where(lo == 0, pair_in, first_decay[:, part] * pair_in + recv_a[:, part])
        sent = jnp.where(lo == 0, first_decay[:, part] * pair_in + own_half[:, part], pair_in)
        recv_c = lax.ppermute(sent, "fl", swap)
        incoming = jnp.where(
            lo == 0, jnp.stack([own_in, recv_c], axis=1), jnp.stack([recv_c, own_in], axis=1)
        )
        base = intra_out.reshape(nck, chunk, group_count, 2, half, HEAD_DIM)[:, :, :, :, part]
        if by_chunk:
            carried = jnp.einsum("ktgn,ghrpn->kghrpt", c32, incoming, precision=exact)
            scale = jnp.transpose(grow[:, :, part], (3, 0, 1, 2, 4))[:, :, :, :, None, :]
            return jnp.transpose(base, (0, 2, 3, 4, 5, 1)) + scale * carried
        carried = jnp.einsum("ktgn,ghrpn->ktghrp", c32, incoming, precision=exact)
        scale = jnp.transpose(grow[:, :, part], (3, 4, 0, 1, 2))[..., None]
        return (base + scale * carried).reshape(row_count, -1)

    first_in, output = exclusive_scan(
        pair_state[:, :first_size], pair_log_half[:, :first_size], pair_count,
        (values32, b_part, c_part, local_list), intra,
    )

    def first_rows(side):
        first_in, output = side
        return finish(first_in, 0, output)

    second_in, first_piece = exclusive_scan(
        pair_state[:, first_size:], pair_log_half[:, first_size:], pair_count,
        (first_in, output), first_rows,
    )
    second_piece = finish(second_in, 1, output)
    if by_chunk:
        firsts = exchange_chunks(first_piece, tp_count)
        seconds = exchange_chunks(second_piece, tp_count)
        blocks = jnp.stack(
            [jnp.concatenate([a, b], axis=2) for a, b in zip(firsts, seconds)], axis=0
        )
        return jnp.transpose(blocks, (5, 0, 1, 2, 3, 4)).reshape(chunk, tp_count * head_count * HEAD_DIM)
    sent_first = exchange_rows(first_piece, tp_count)
    sent_second = exchange_rows(second_piece, tp_count)
    rows = row_count // tp_count
    both = [
        piece.reshape(rows, tp_count, group_count, 2, size, HEAD_DIM)
        for piece, size in zip((sent_first, sent_second), sizes)
    ]
    return jnp.concatenate(both, axis=4).reshape(rows, tp_count * head_count * HEAD_DIM)


def exclusive_scan(state, log_decay, count, side, work):
    shape = state.shape
    width = state.shape[-1]
    heads = log_decay.size
    per_head = state.size // heads // width
    log_rows = -(-heads // width)

    def shifted(value, step):
        return lax.ppermute(value, "fh", [(d, d + step) for d in range(count - step)])

    def combine(got, cur):
        scale = jnp.repeat(jnp.exp(cur[-log_rows:].reshape(-1)[:heads]), per_head)[:, None]
        body = scale * got[:-log_rows] + cur[:-log_rows]
        logs = got[-log_rows:] + cur[-log_rows:]
        return jnp.concatenate([body, logs], axis=0)

    flat_log = jnp.pad(log_decay.reshape(-1), (0, log_rows * width - heads)).reshape(log_rows, width)
    first = jnp.concatenate([state.reshape(-1, width), flat_log], axis=0)
    first, side = lax.optimization_barrier((first, side))
    cur = shifted(first, 1)
    done = work(side)
    cur, done = lax.optimization_barrier((cur, done))
    window = combine(cur, first)
    step = 2
    while step < count:
        got = shifted(window, step)
        cur = combine(got, cur)
        if 2 * step < count:
            window = combine(got, window)
        step *= 2
    return cur[:-log_rows].reshape(shape), done


def exchange_chunks(piece, tp_count):
    mine = lax.axis_index("tp")
    pieces = [None] * tp_count
    for shift in range(tp_count):
        sent = lax.dynamic_index_in_dim(piece, (mine + shift) % tp_count, 0, keepdims=False)
        if shift == 0:
            pieces[shift] = sent
        else:
            pieces[shift] = lax.ppermute(
                sent, "tp", [(d, (d + shift) % tp_count) for d in range(tp_count)]
            )
    placed = []
    for column in range(tp_count):
        value = pieces[0]
        for shift in range(1, tp_count):
            value = jnp.where((mine - shift) % tp_count == column, pieces[shift], value)
        placed.append(value)
    return placed


def exchange_rows(merged, tp_count):
    mine = lax.axis_index("tp")
    rows = merged.shape[0] // tp_count
    blocks = merged.reshape(tp_count, rows, merged.shape[1])
    pieces = [None] * tp_count
    for shift in range(tp_count):
        sent = lax.dynamic_index_in_dim(blocks, (mine + shift) % tp_count, 0, keepdims=False)
        if shift == 0:
            got = sent
        else:
            got = lax.ppermute(sent, "tp", [(d, (d + shift) % tp_count) for d in range(tp_count)])
        pieces[shift] = got
    placed = []
    for column in range(tp_count):
        value = pieces[0]
        for shift in range(1, tp_count):
            value = jnp.where((mine - shift) % tp_count == column, pieces[shift], value)
        placed.append(value)
    return jnp.concatenate(placed, axis=1)


def solution(mesh):
    seq_count = mesh.shape["fsdp"]
    tp_count = mesh.shape["tp"]
    grid = Mesh(mesh.devices.reshape(seq_count // 2, 2, tp_count), ("fh", "fl", "tp"))
    in_specs = (
        P(SEQ, "tp", None),
        P("tp", SEQ),
        P(None, "tp", None),
        P("tp", None),
        P("tp"),
        P("tp"),
        P("tp"),
    )
    out_specs = P(SEQ + ("tp",), None)

    def body(*args):
        return shards(*args, seq_count=seq_count, tp_count=tp_count)

    return jax.shard_map(body, mesh=grid, in_specs=in_specs, out_specs=out_specs, check_vma=False)
```

profile of v0, /device:TPU:24, one launch (start us, length us, event | category | flops | bytes accessed | tf_op | source)
XLA Modules:
  0.0 399.4 jit_solution(843596547263673128)
XLA Ops:
  0.0 3.0 copy.24
  3.0 2.2 copy-done.1
  5.2 1.9 collective-permute-start.1
  7.6 2.3 reduce_window_sum.24
  10.5 1.3 collective-permute-done.1
  11.8 13.7 %multiply_convert_fusion = bf16[256,4,2304]{2,0,1:T(8,128)(2,1)S(1)} fusion(bf16[256,4,2304]{2,0,1:T(8,128)(2,1)} %copy-done.1, bf16[3,4,2304]{2,0,1:T(4,128)(2,1)S(1)} %collective-permute-done.1, f32[4,2304]{1,0:T(4,128)S(1)} %get-tuple-element.49, f32[4,2304]{1,0:T(4,128)S(1)} %get-tuple-element.50, f32[4,2304]{1,0:T(4,128)S(1)} %get-tuple-element.48, ...), kind=kLoop, calls=%fused_computation.6 | loop fusion | flops 61341696 | bytes 9676800 | tf_op jit(solution)/shard_map/convert_element_type | solution.py:22
  25.6 2.6 slice.262
  28.2 6.2 %copy.27 = bf16[256,4,2048]{0,2,1:T(8,128)(2,1)} copy(bf16[256,4,2048]{2,0,1:T(8,128)(2,1)} %slice.262) | data formatting | bytes 8388608 | tf_op jit(solution)/shard_map/slice | solution.py:36
  34.4 6.9 %reshape.122 = bf16[2,128,4,32,64]{1,0,4,3,2:T(2,128)(2,1)} reshape(bf16[256,4,2048]{0,2,1:T(8,128)(2,1)} %copy.27) | data formatting | bytes 8388608 | tf_op jit(solution)/shard_map/reshape | solution.py:36
  41.4 10.5 %convert_multiply_fusion = f32[2,128,4,32,64]{1,0,4,3,2:T(2,128)} fusion(bf16[2,128,4,32,64]{1,0,4,3,2:T(2,128)(2,1)} %reshape.122, f32[2,128,4,32]{1,0,3,2:T(2,128)S(1)} %copy.30), kind=kLoop, calls=%fused_computation.17 | loop fusion | flops 4194304 | bytes 12713984 | tf_op jit(solution)/shard_map/mul | solution.py:49
  51.9 7.4 %fusion.6 = f32[2,4,32,64,128]{4,3,2,1,0:T(8,128)S(1)} fusion(f32[2,128,4,32,64]{1,0,4,3,2:T(2,128)} %convert_multiply_fusion, bf16[2,128,4,128,1]{3,1,0,2,4:T(8,128)(2,1)S(1)} %bitcast.160), kind=kOutput, calls=%fused_computation.10 | convolution fusion | flops 3221225472 | bytes 17039360 | tf_op jit(solution)/shard_map/ksgn,ksgjp->kgjpn/dot_general | solution.py:50
  59.3 2.5 fusion.17
  61.7 2.0 copy-done
  63.7 1.5 constant_dynamic-slice_fusion.1
  68.3 1.3 collective-permute-done
  69.7 2.7 select_add_fusion
  72.5 1.3 copy-done.3
  74.1 2.7 collective-permute-start.3
  77.6 1.2 convolution_bitcast_fusion
  78.8 22.4 %bitcast_add_fusion = f32[2,128,4,32,64]{1,4,3,2,0:T(8,128)} fusion(f32[4,32]{1,0:T(4,128)} %mul.308, bf16[2,128,4,32,64]{1,0,4,3,2:T(2,128)(2,1)} %reshape.122, f32[4,32,2,128]{3,1,0,2:T(8,128)} %copy.35, f32[4,2,128,128]{3,2,0,1:T(8,128)S(1)} %convolution_bitcast_fusion, pred[128,128]{1,0:T(8,128)(4,1)} %iota_compare_fusion, ...), kind=kOutput, calls=%fused_computation.9 | convolution fusion | flops 3244294144 | bytes 13386240 | tf_op jit(solution)/shard_map/gjkts,ksgjp->ktgjp/dot_general | solution.py:72
  101.3 2.2 copy-done.2
  103.4 4.2 %slice_add_fusion = f32[1,128,4,32,64]{1,4,3,2,0:T(8,128)S(1)} fusion(f32[2,128,4,32,64]{1,4,3,2,0:T(8,128)} %bitcast_add_fusion, f32[4,32,64,128]{3,2,1,0:T(8,128)S(1)} %copy-done.2, f32[128,4,32]{0,2,1:T(8,128)S(1)} %copy-done.8, bf16[2,128,4,128]{3,1,0,2:T(8,128)(2,1)S(1)} %bitcast.156), kind=kOutput, calls=%fused_computation.27 | convolution fusion | flops 1612709888 | bytes 12779520 | tf_op jit(solution)/shard_map/ktgn,kgjpn->ktgjp/dot_general | solution.py:78
  107.7 4.2 %pad_maximum_fusion = f32[2,128,4,32,64]{1,4,3,2,0:T(8,128)} fusion(f32[1,128,4,32,64]{1,4,3,2,0:T(8,128)S(1)} %slice_add_fusion, f32[1,128,4,32,64]{1,4,3,2,0:T(8,128)S(1)} %slice-done), kind=kLoop, calls=%fused_computation.7 | loop fusion | flops 2097152 | bytes 16777216 | tf_op jit(solution)/shard_map/concatenate | solution.py:80
  111.9 1.8 collective-permute-done.3
  113.7 0.7 slice_add_fusion.6
  114.4 1.9 slice_add_fusion.2
  116.3 1.3 pad_maximum_fusion.4
  117.5 1.3 collective-permute-start.4
  119.5 1.4 mul.317
  120.9 34.5 %collective-permute-done.4 = f32[3073,128]{1,0:T(8,128)S(1)} collective-permute-done((f32[3073,128]{1,0:T(8,128)}, f32[3073,128]{1,0:T(8,128)S(1)}, u32[]{:S(2)}, u32[]{:S(2)}) %collective-permute-start.4) | collective-permute-done | bytes 1573408 | tf_op jit(solution)/shard_map/ppermute | solution.py:162
  155.5 1.1 copy-done.5
  156.6 1.3 slice_add_fusion.10
  157.9 1.9 multiply_add_fusion
  159.8 1.2 pad_maximum_fusion.5
  161.1 1.3 collective-permute-start.5
  162.6 0.7 exponential_bitcast_fusion.5
  163.5 69.3 %collective-permute-done.5 = f32[3073,128]{1,0:T(8,128)} collective-permute-done((f32[3073,128]{1,0:T(8,128)}, f32[3073,128]{1,0:T(8,128)}, u32[]{:S(2)}, u32[]{:S(2)}) %collective-permute-start.5) | collective-permute-done | bytes 1573408 | tf_op jit(solution)/shard_map/ppermute | solution.py:162
  232.8 3.3 fusion.33
  236.2 3.4 fusion.32
  240.1 2.6 collective-permute-start.6
  243.3 9.3 %fusion.14 = f32[2,4,2,12,64,128]{5,4,0,3,2,1:T(8,128)} fusion(f32[2,4,2,12,128]{4,0,3,2,1:T(2,128)S(1)} %slice_bitcast_fusion.4, bf16[2,128,4,128,1,1]{3,1,0,5,4,2:T(8,128)(2,1)S(1)} %bitcast.157, f32[2,128,4,2,16,64]{1,5,4,3,2,0:T(8,128)} %bitcast.149, f32[4,1,12,64,128]{4,3,2,0,1:T(8,128)} %bitcast.39, f32[4,1,12,64,128]{4,3,2,0,1:T(8,128)S(1)} %get-tuple-element.39, ...), kind=kOutput, calls=%fused_computation.22 | convolution fusion | flops 2421424128 | bytes 16089089 | tf_op jit(solution)/shard_map/ktgn,ghrpn->kghrpt/dot_general | solution.py:116
  252.6 4.8 %collective-permute-done.6 = f32[1025,128]{1,0:T(8,128)} collective-permute-done((f32[1025,128]{1,0:T(8,128)S(1)}, f32[1025,128]{1,0:T(8,128)}, u32[]{:S(2)}, u32[]{:S(2)}) %collective-permute-start.6) | collective-permute-done | bytes 524832 | tf_op jit(solution)/shard_map/ppermute | solution.py:162
  257.4 0.7 slice_add_fusion.5
  258.1 1.2 slice_add_fusion.4
  259.3 1.3 collective-permute-start.9
  260.9 13.9 %collective-permute-done.9 = f32[1025,128]{1,0:T(8,128)S(1)} collective-permute-done((f32[1025,128]{1,0:T(8,128)S(1)}, f32[1025,128]{1,0:T(8,128)S(1)}, u32[]{:S(2)}, u32[]{:S(2)}) %collective-permute-start.9) | collective-permute-done | bytes 524832 | tf_op jit(solution)/shard_map/ppermute | solution.py:162
  274.8 0.7 slice_add_fusion.8
  275.7 1.3 collective-permute-start.10
  277.0 4.0 dynamic-slice_bitcast_fusion
  281.0 1.5 collective-permute-start.8
  282.5 0.7 exponential_bitcast_fusion.1
  283.5 18.0 %collective-permute-done.10 = f32[1025,128]{1,0:T(8,128)S(1)} collective-permute-done((f32[1025,128]{1,0:T(8,128)S(1)}, f32[1025,128]{1,0:T(8,128)S(1)}, u32[]{:S(2)}, u32[]{:S(2)}) %collective-permute-start.10) | collective-permute-done | bytes 524832 | tf_op jit(solution)/shard_map/ppermute | solution.py:162
  301.5 1.4 fusion.39
  302.9 1.4 fusion.38
  304.4 0.8 slice_bitcast_fusion.5
  305.1 1.1 collective-permute-done.11
  306.3 2.7 fusion.29
  309.1 1.6 collective-permute-start.12
  310.6 62.0 %collective-permute-done.12 = f32[4,2,4,64,128]{4,3,2,1,0:T(8,128)} collective-permute-done((f32[4,2,4,64,128]{4,3,2,1,0:T(8,128)S(1)}, f32[4,2,4,64,128]{4,3,2,1,0:T(8,128)}, u32[]{:S(2)}, u32[]{:S(2)}) %collective-permute-start.12) | collective-permute-done | bytes 1048608 | tf_op jit(solution)/shard_map/ppermute | solution.py:195
  372.6 2.4 bitcast_select_fusion.3
  375.0 6.9 %bitcast_select_fusion.1 = (f32[4,2,12,64,128]{4,3,2,1,0:T(8,128)}, f32[4,2,12,64,128]{4,3,2,1,0:T(8,128)}) fusion(f32[4,2,12,64,128]{4,3,2,1,0:T(8,128)} %collective-permute-done.8, f32[2,4,2,12,64,128]{5,4,0,3,2,1:T(8,128)} %fusion.14, s32[]{:T(128)S(6)} %select_n.159, pred[]{:T(512)S(6)} %eq.15, pred[]{:T(512)S(6)} %eq.31), kind=kLoop, calls=%fused_computation.39 | loop fusion | flops 1572864 | bytes 12582918 | tf_op jit(solution)/shard_map/jit(_where)/select_n | solution.py:202
  381.9 4.1 %maximum_bitcast_fusion = (f32[1,4,2,16,64,128]{5,4,3,2,1,0:T(8,128)S(1)}, f32[1,4,2,16,64,128]{5,4,3,2,1,0:T(8,128)S(1)}) fusion(f32[4,2,4,64,128]{4,3,2,1,0:T(8,128)S(1)} %get-tuple-element.35, f32[4,2,12,64,128]{4,3,2,1,0:T(8,128)} %get-tuple-element.31, f32[4,2,4,64,128]{4,3,2,1,0:T(8,128)} %get-tuple-element.36, f32[4,2,12,64,128]{4,3,2,1,0:T(8,128)} %get-tuple-element.32), kind=kLoop, calls=%fused_computation.32 | loop fusion | flops 2097152 | bytes 16777216 | tf_op jit(solution)/shard_map/stack | solution.py:140
  386.0 4.4 %pad_maximum_fusion.1 = f32[2,4,2,16,64,128]{5,4,3,2,1,0:T(8,128)} fusion(f32[1,4,2,16,64,128]{5,4,3,2,1,0:T(8,128)S(1)} %get-tuple-element.61, f32[1,4,2,16,64,128]{5,4,3,2,1,0:T(8,128)S(1)} %get-tuple-element.60), kind=kLoop, calls=%fused_computation.8 | loop fusion | flops 2097152 | bytes 16777216 | tf_op jit(solution)/shard_map/stack | solution.py:140
  390.4 9.0 %copy.45 = f32[128,16384]{1,0:T(8,128)} copy(f32[128,16384]{0,1:T(8,128)} %bitcast.151) | data formatting | bytes 16777216 | tf_op jit(solution)/shard_map/reshape | solution.py:143
  (104 shorter events, 8.6 us)
Async XLA Ops:
  0.0 7.2 %copy-start.17 = (f32[128]{0:T(128)S(1)}, f32[128]{0:T(128)}, u32[]{:S(2)}) copy-start(f32[128]{0:T(128)} %param.12) | copy-start | bytes 1540
  0.0 7.2 %copy-start.9 = (bf16[4,4,2304]{2,1,0:T(4,128)(2,1)S(1)}, bf16[4,4,2304]{2,1,0:T(4,128)(2,1)}, u32[]{:S(2)}) copy-start(bf16[4,4,2304]{2,1,0:T(4,128)(2,1)} %param.9) | copy-start | bytes 221188
  0.0 7.2 %copy-start.14 = (f32[128]{0:T(128)S(1)}, f32[128]{0:T(128)}, u32[]{:S(2)}) copy-start(f32[128]{0:T(128)} %param.11) | copy-start | bytes 1540
  0.0 7.2 %copy-start.10 = (bf16[128,256]{1,0:T(8,128)(2,1)S(1)}, bf16[128,256]{1,0:T(8,128)(2,1)}, u32[]{:S(2)}) copy-start(bf16[128,256]{1,0:T(8,128)(2,1)} %param.8) | copy-start | bytes 196612
  0.0 10.3 %copy-start.12 = (bf16[4,2304]{1,0:T(4,128)(2,1)S(1)}, bf16[4,2304]{1,0:T(4,128)(2,1)}, u32[]{:S(2)}) copy-start(bf16[4,2304]{1,0:T(4,128)(2,1)} %param.10) | copy-start | bytes 55300
  3.0 2.2 copy-start.1
  5.2 6.6 %collective-permute-start.1 = (bf16[3,4,2304]{2,0,1:T(4,128)(2,1)S(1)}, bf16[3,4,2304]{2,0,1:T(4,128)(2,1)S(1)}, u32[]{:S(2)}, u32[]{:S(2)}) collective-permute-start(bf16[3,4,2304]{2,0,1:T(4,128)(2,1)S(1)} %slice.257), channel_id=1, source_target_pairs={{0,2},{2,4},{4,6},{6,8},{8,10},{10,12},{12,14},{14,16},{16,18},{18... | collective-permute-start | bytes 165896 | tf_op jit(solution)/shard_map/ppermute | solution.py:15
  25.6 26.2 %copy-start.6 = (bf16[256,4,128]{2,0,1:T(8,128)(2,1)}, bf16[256,4,128]{2,0,1:T(8,128)(2,1)S(1)}, u32[]{:S(2)}) copy-start(bf16[256,4,128]{2,0,1:T(8,128)(2,1)S(1)} %get-tuple-element.34) | copy-start | bytes 786436
  61.7 2.0 copy-start
  61.7 5.9 %copy-start.15 = (f32[128]{0:T(128)S(1)}, f32[128]{0:T(128)}, u32[]{:S(2)}) copy-start(f32[128]{0:T(128)} %param.13) | copy-start | bytes 1540
  65.2 4.6 %collective-permute-start.2 = (f32[4,16,64,128]{3,2,1,0:T(8,128)}, f32[4,16,64,128]{3,2,1,0:T(8,128)S(1)}, u32[]{:S(2)}, u32[]{:S(2)}) collective-permute-start(f32[4,16,64,128]{3,2,1,0:T(8,128)} %constant_dynamic-slice_fusion.1), channel_id=1, source_target_pairs={{0,2},{2,0},{1,3},{3,1},{4,6},{6,4},{5,7},{7,5},{8,10},{10,8},{9,1... | collective-permute-start | bytes 6291464 | tf_op jit(solution)/shard_map/ppermute | solution.py:91
  65.5 4.1 %collective-permute-start = (f32[4,32]{1,0:T(4,128)S(1)}, f32[4,32]{1,0:T(4,128)S(1)}, u32[]{:S(2)}, u32[]{:S(2)}) collective-permute-start(f32[4,32]{1,0:T(4,128)S(1)} %get-tuple-element.46), channel_id=1, source_target_pairs={{0,2},{2,0},{1,3},{3,1},{4,6},{6,4},{5,7},{7,5},{8,10},{10,8},{9,1... | collective-permute-start | bytes 1544 | tf_op jit(solution)/shard_map/ppermute | solution.py:86
  69.7 4.3 %copy-start.4 = (f32[4,16,64,128]{3,2,1,0:T(8,128)}, f32[4,16,64,128]{3,2,1,0:T(8,128)S(1)}, u32[]{:S(2)}) copy-start(f32[4,16,64,128]{3,2,1,0:T(8,128)S(1)} %collective-permute-done.2) | copy-start | bytes 6291460
  72.5 1.4 copy-start.3
  74.1 39.6 %collective-permute-start.3 = (f32[3073,128]{1,0:T(8,128)S(1)}, f32[3073,128]{1,0:T(8,128)}, u32[]{:S(2)}, u32[]{:S(2)}) collective-permute-start(f32[3073,128]{1,0:T(8,128)S(1)} %pad_maximum_fusion.3), channel_id=1, source_target_pairs={{0,4},{4,8},{8,12},{12,16},{16,20},{20,24},{24,28},{1,5},{5,9},{9,... | collective-permute-start | bytes 4720136 | tf_op jit(solution)/shard_map/ppermute | solution.py:162
  101.2 2.2 copy-start.2
  101.2 2.2 copy-start.8
  103.4 4.2 %slice-start = ((f32[2,128,4,32,64]{1,4,3,2,0:T(8,128)}), f32[1,128,4,32,64]{1,4,3,2,0:T(8,128)S(1)}, s32[]{:S(2)}) async-start(f32[2,128,4,32,64]{1,4,3,2,0:T(8,128)} %bitcast_add_fusion), calls=%async_computation | async-start | bytes 8388608 | tf_op jit(solution)/shard_map/slice | solution.py:80
  107.6 6.7 %copy-start.11 = (f32[3072]{0:T(1024)S(1)}, f32[3072]{0:T(1024)}, u32[]{:S(2)}) copy-start(f32[3072]{0:T(1024)} %mul.302) | copy-start | bytes 36868
  114.4 4.4 %copy-start.13 = (f32[1,128]{1,0:T(1,128)}, f32[1,128]{1,0:T(1,128)S(1)}, u32[]{:S(2)}) copy-start(f32[1,128]{1,0:T(1,128)S(1)} %slice_add_fusion.6) | copy-start | bytes 1540
  117.5 37.9 %collective-permute-start.4 = (f32[3073,128]{1,0:T(8,128)}, f32[3073,128]{1,0:T(8,128)S(1)}, u32[]{:S(2)}, u32[]{:S(2)}) collective-permute-start(f32[3073,128]{1,0:T(8,128)} %pad_maximum_fusion.4), channel_id=1, source_target_pairs={{0,8},{4,12},{8,16},{12,20},{16,24},{20,28},{1,9},{5,13},{9,17},{1... | collective-permute-start | bytes 4720136 | tf_op jit(solution)/shard_map/ppermute | solution.py:162
  155.5 1.2 copy-start.5
  157.9 4.6 %slice-start.1 = ((f32[4,16,64,128]{3,2,1,0:T(8,128)}), f32[4,4,64,128]{3,2,1,0:T(8,128)S(1)}, s32[]{:S(2)}) async-start(f32[4,16,64,128]{3,2,1,0:T(8,128)} %copy-done.3), calls=%async_computation.1 | async-start | bytes 1048576 | tf_op jit(solution)/shard_map/slice | solution.py:133
  157.9 5.5 %copy-start.16 = (f32[1,128]{1,0:T(1,128)S(1)}, f32[1,128]{1,0:T(1,128)}, u32[]{:S(2)}) copy-start(f32[1,128]{1,0:T(1,128)} %get-tuple-element.37) | copy-start | bytes 1540
  161.1 71.8 %collective-permute-start.5 = (f32[3073,128]{1,0:T(8,128)}, f32[3073,128]{1,0:T(8,128)}, u32[]{:S(2)}, u32[]{:S(2)}) collective-permute-start(f32[3073,128]{1,0:T(8,128)} %pad_maximum_fusion.5), channel_id=1, source_target_pairs={{0,16},{4,20},{8,24},{12,28},{1,17},{5,21},{9,25},{13,29},{2,18},{... | collective-permute-start | bytes 4720136 | tf_op jit(solution)/shard_map/ppermute | solution.py:162
  239.6 3.8 collective-permute-start.7
  240.0 12.6 %copy-start.7 = (f32[4,2,16,2,128]{4,3,2,1,0:T(2,128)}, f32[4,2,16,2,128]{4,3,2,1,0:T(2,128)S(1)}, u32[]{:S(2)}) copy-start(f32[4,2,16,2,128]{4,3,2,1,0:T(2,128)S(1)} %fusion.42) | copy-start | bytes 393220
  240.1 17.3 %collective-permute-start.6 = (f32[1025,128]{1,0:T(8,128)S(1)}, f32[1025,128]{1,0:T(8,128)}, u32[]{:S(2)}, u32[]{:S(2)}) collective-permute-start(f32[1025,128]{1,0:T(8,128)S(1)} %pad_maximum_fusion.6), channel_id=1, source_target_pairs={{0,4},{4,8},{8,12},{12,16},{16,20},{20,24},{24,28},{1,5},{5,9},{9,... | collective-permute-start | bytes 1574408 | tf_op jit(solution)/shard_map/ppermute | solution.py:162
  259.3 15.4 %collective-permute-start.9 = (f32[1025,128]{1,0:T(8,128)S(1)}, f32[1025,128]{1,0:T(8,128)S(1)}, u32[]{:S(2)}, u32[]{:S(2)}) collective-permute-start(f32[1025,128]{1,0:T(8,128)S(1)} %pad_maximum_fusion.7), channel_id=1, source_target_pairs={{0,8},{4,12},{8,16},{12,20},{16,24},{20,28},{1,9},{5,13},{9,17},{1... | collective-permute-start | bytes 1574408 | tf_op jit(solution)/shard_map/ppermute | solution.py:162
  275.7 25.8 %collective-permute-start.10 = (f32[1025,128]{1,0:T(8,128)S(1)}, f32[1025,128]{1,0:T(8,128)S(1)}, u32[]{:S(2)}, u32[]{:S(2)}) collective-permute-start(f32[1025,128]{1,0:T(8,128)S(1)} %pad_maximum_fusion.8), channel_id=1, source_target_pairs={{0,16},{4,20},{8,24},{12,28},{1,17},{5,21},{9,25},{13,29},{2,18},{... | collective-permute-start | bytes 1574408 | tf_op jit(solution)/shard_map/ppermute | solution.py:162
  281.0 94.0 %collective-permute-start.8 = (f32[4,2,12,64,128]{4,3,2,1,0:T(8,128)}, f32[4,2,12,64,128]{4,3,2,1,0:T(8,128)}, u32[]{:S(2)}, u32[]{:S(2)}) collective-permute-start(f32[4,2,12,64,128]{4,3,2,1,0:T(8,128)} %dynamic-slice_bitcast_fusion), channel_id=1, source_target_pairs={{0,1},{1,0},{2,3},{3,2},{4,5},{5,4},{6,7},{7,6},{8,9},{9,8},{10,11... | collective-permute-start | bytes 9437192 | tf_op jit(solution)/shard_map/ppermute | solution.py:195
  304.3 2.0 collective-permute-start.11
  309.1 63.5 %collective-permute-start.12 = (f32[4,2,4,64,128]{4,3,2,1,0:T(8,128)S(1)}, f32[4,2,4,64,128]{4,3,2,1,0:T(8,128)}, u32[]{:S(2)}, u32[]{:S(2)}) collective-permute-start(f32[4,2,4,64,128]{4,3,2,1,0:T(8,128)S(1)} %dynamic-slice_bitcast_fusion.1), channel_id=1, source_target_pairs={{0,1},{1,0},{2,3},{3,2},{4,5},{5,4},{6,7},{7,6},{8,9},{9,8},{10,11... | collective-permute-start | bytes 3145736 | tf_op jit(solution)/shard_map/ppermute | solution.py:195
where the time goes:
time: 404 us; the launch traced here: 399 us
  waiting for transfers between devices  209 us (52%)
  other arithmetic  76 us (19%)
  local copies, waits for them, and re-layouts  51.2 us (13%)
  matrix products  47.2 us (12%)
  starting transfers between devices  16 us (4%)
    ppermute x6, waiting for transfers between devices, shifted(): lax.ppermute(value, 'fh', [(d, d + step) for d in range(count - step)])  142 us
    ppermute x2, waiting for transfers between devices, exchange_chunks(): lax.ppermute(sent, 'tp', [(d, (d + shift) % tp_count) for d in range(tp_c...  62 us
    dot_general x1, matrix products, intra(): output = jnp.einsum('gjkts,ksgjp->ktgjp', mixing, values32, precision=exact)  22.4 us
    convert_element_type x1, other arithmetic, convolve(): return jax.nn.silu(summed).astype(jnp.bfloat16)  13.7 us
    unnamed x38, local copies, waits for them, and re-layouts  12 us
    dot_general x2, matrix products, finish(): carried = jnp.einsum('ktgn,ghrpn->kghrpt', c32, incoming, precision=exact)  11.9 us
    mul x1, other arithmetic, shards(): weighted = values32 * jnp.transpose(weights, (2, 3, 0, 1))[..., None]  10.5 us
    ppermute x6, starting transfers between devices, shifted(): lax.ppermute(value, 'fh', [(d, d + step) for d in range(count - step)])  10.4 us
  transfers between devices with their start and end apart: 13, of which 11 were waited for; matrix products, arithmetic and copies ran while one was open for 16% of the time, Pallas kernels for 0%

commit v1 on v0

--- a/solution.py
+++ b/solution.py
@@ -113,10 +113,10 @@
         )
         base = intra_out.reshape(nck, chunk, group_count, 2, half, HEAD_DIM)[:, :, :, :, part]
         if by_chunk:
-            carried = jnp.einsum("ktgn,ghrpn->kghrpt", c32, incoming, precision=exact)
+            carried = jnp.einsum("ktgn,ghrpn->kghrpt", c32, incoming, precision=lax.Precision.HIGH)
             scale = jnp.transpose(grow[:, :, part], (3, 0, 1, 2, 4))[:, :, :, :, None, :]
             return jnp.transpose(base, (0, 2, 3, 4, 5, 1)) + scale * carried
-        carried = jnp.einsum("ktgn,ghrpn->ktghrp", c32, incoming, precision=exact)
+        carried = jnp.einsum("ktgn,ghrpn->ktghrp", c32, incoming, precision=lax.Precision.HIGH)
         scale = jnp.transpose(grow[:, :, part], (3, 4, 0, 1, 2))[..., None]
         return (base + scale * carried).reshape(row_count, -1)
 
@@ -137,9 +137,12 @@
     if by_chunk:
         firsts = exchange_chunks(first_piece, tp_count)
         seconds = exchange_chunks(second_piece, tp_count)
-        blocks = jnp.stack(
-            [jnp.concatenate([a, b], axis=2) for a, b in zip(firsts, seconds)], axis=0
-        )
+        mine = lax.axis_index("tp")
+        by_shift = [jnp.concatenate([a, b], axis=2)[None] for a, b in zip(firsts, seconds)]
+        column = lax.broadcasted_iota(jnp.int32, (tp_count,) + (1,) * (by_shift[0].ndim - 1), 0)
+        blocks = by_shift[0]
+        for shift in range(1, tp_count):
+            blocks = jnp.where((mine - shift) % tp_count == column, by_shift[shift], blocks)
         return jnp.transpose(blocks, (5, 0, 1, 2, 3, 4)).reshape(chunk, tp_count * head_count * HEAD_DIM)
     sent_first = exchange_rows(first_piece, tp_count)
     sent_second = exchange_rows(second_piece, tp_count)
@@ -195,13 +198,7 @@
             pieces[shift] = lax.ppermute(
                 sent, "tp", [(d, (d + shift) % tp_count) for d in range(tp_count)]
             )
-    placed = []
-    for column in range(tp_count):
-        value = pieces[0]
-        for shift in range(1, tp_count):
-            value = jnp.where((mine - shift) % tp_count == column, pieces[shift], value)
-        placed.append(value)
-    return placed
+    return pieces
 
 
 def exchange_rows(merged, tp_count):

time: 404 us -> 382 us (0.946)
  waiting for transfers between devices: 209 us -> 192 us
  other arithmetic: 76 us -> 69.6 us
    ppermute x2, waiting for transfers between devices: 62 us -> 42.5 us  [exchange_chunks(): lax.ppermute(sent, 'tp', [(d, (d + shift) % tp_count) for d in range(tp_c...]
    reshape x1 -> x0, local copies, waits for them, and re-layouts: 8.99 us -> none  [shards(): jnp.transpose(blocks, (5, 0, 1, 2, 3, 4))]
    select_n x0 -> x1, local copies, waits for them, and re-layouts: none -> 8.99 us  [shards(): jnp.where((mine - shift) % tp_count == column, by_shift[shift], blocks)]
    another operation x2 -> x0, other arithmetic: 8.47 us -> none  [shards(): jnp.stack([jnp.concatenate([a, b], axis=2) for a, b in zip(firsts, second...]
    select_n x2 -> x1, other arithmetic: 9.32 us -> 4.48 us  [shards(): jnp.where((mine - shift) % tp_count == column, by_shift[shift], blocks)]
    broadcast_in_dim x0 -> x2, other arithmetic: none -> 4.06 us  [shards(): jnp.where((mine - shift) % tp_count == column, by_shift[shift], blocks)]
    unnamed x38 -> x44, local copies, waits for them, and re-layouts: 12 us -> 10.8 us
  transfers between devices with their start and end apart: 13 -> 13, of which waited for: 11 -> 11; matrix products, arithmetic and copies ran while one was open for 16% -> 19% of each run, Pallas kernels for 0% -> 0%
where the time goes in v1:
time: 382 us; the launch traced here: 377 us
  waiting for transfers between devices  192 us (50%)
  other arithmetic  69.6 us (18%)
  local copies, waits for them, and re-layouts  53.2 us (14%)
  matrix products  46.2 us (12%)
  starting transfers between devices  15.8 us (4%)
    ppermute x6, waiting for transfers between devices, shifted(): lax.ppermute(value, 'fh', [(d, d + step) for d in range(count - step)])  144 us
    ppermute x2, waiting for transfers between devices, exchange_chunks(): lax.ppermute(sent, 'tp', [(d, (d + shift) % tp_count) for d in range(tp_c...  42.5 us
    dot_general x1, matrix products, intra(): output = jnp.einsum('gjkts,ksgjp->ktgjp', mixing, values32, precision=exact)  21.5 us
    convert_element_type x1, other arithmetic, convolve(): return jax.nn.silu(summed).astype(jnp.bfloat16)  13.7 us
    add x6, other arithmetic, combine(): body = scale * got[:-log_rows] + cur[:-log_rows]  11.3 us
    dot_general x2, matrix products, finish(): jnp.einsum('ktgn,ghrpn->kghrpt', c32, incoming, precision=lax.Precision.H...  10.9 us
    unnamed x44, local copies, waits for them, and re-layouts  10.8 us
    mul x1, other arithmetic, shards(): weighted = values32 * jnp.transpose(weights, (2, 3, 0, 1))[..., None]  10.5 us
  transfers between devices with their start and end apart: 13, of which 11 were waited for; matrix products, arithmetic and copies ran while one was open for 19% of the time, Pallas kernels for 0%

profile of v1, /device:TPU:24, one launch (start us, length us, event | category | flops | bytes accessed | tf_op | source)
XLA Modules:
  0.0 377.0 jit_solution(10673423972091918584)
XLA Ops:
  0.0 3.0 copy.24
  3.0 2.2 copy-done.1
  5.3 1.9 collective-permute-start.1
  7.5 2.3 reduce_window_sum.24
  10.5 1.3 collective-permute-done.1
  11.8 13.7 %multiply_convert_fusion = bf16[256,4,2304]{2,0,1:T(8,128)(2,1)S(1)} fusion(bf16[256,4,2304]{2,0,1:T(8,128)(2,1)} %copy-done.1, bf16[3,4,2304]{2,0,1:T(4,128)(2,1)S(1)} %collective-permute-done.1, f32[4,2304]{1,0:T(4,128)S(1)} %get-tuple-element.49, f32[4,2304]{1,0:T(4,128)S(1)} %get-tuple-element.50, f32[4,2304]{1,0:T(4,128)S(1)} %get-tuple-element.48, ...), kind=kLoop, calls=%fused_computation.6 | loop fusion | flops 61341696 | bytes 9676800 | tf_op jit(solution)/shard_map/convert_element_type | solution.py:22
  25.5 2.6 slice.262
  28.2 6.3 %copy.27 = bf16[256,4,2048]{0,2,1:T(8,128)(2,1)} copy(bf16[256,4,2048]{2,0,1:T(8,128)(2,1)} %slice.262) | data formatting | bytes 8388608 | tf_op jit(solution)/shard_map/slice | solution.py:36
  34.5 6.9 %reshape.130 = bf16[2,128,4,32,64]{1,0,4,3,2:T(2,128)(2,1)} reshape(bf16[256,4,2048]{0,2,1:T(8,128)(2,1)} %copy.27) | data formatting | bytes 8388608 | tf_op jit(solution)/shard_map/reshape | solution.py:36
  41.4 10.5 %convert_multiply_fusion = f32[2,128,4,32,64]{1,0,4,3,2:T(2,128)} fusion(bf16[2,128,4,32,64]{1,0,4,3,2:T(2,128)(2,1)} %reshape.130, f32[2,128,4,32]{1,0,3,2:T(2,128)S(1)} %copy.30), kind=kLoop, calls=%fused_computation.17 | loop fusion | flops 4194304 | bytes 12713984 | tf_op jit(solution)/shard_map/mul | solution.py:49
  52.0 7.4 %fusion.6 = f32[2,4,32,64,128]{4,3,2,1,0:T(8,128)S(1)} fusion(f32[2,128,4,32,64]{1,0,4,3,2:T(2,128)} %convert_multiply_fusion, bf16[2,128,4,128,1]{3,1,0,2,4:T(8,128)(2,1)S(1)} %bitcast.160), kind=kOutput, calls=%fused_computation.10 | convolution fusion | flops 3221225472 | bytes 17039360 | tf_op jit(solution)/shard_map/ksgn,ksgjp->kgjpn/dot_general | solution.py:50
  59.3 2.4 fusion.17
  61.7 2.1 copy-done
  63.8 1.5 constant_dynamic-slice_fusion.1
  68.4 1.3 collective-permute-done
  69.8 2.7 select_add_fusion
  72.6 1.4 copy-done.3
  74.2 2.9 collective-permute-start.3
  77.5 21.5 %bitcast_add_fusion = f32[2,128,4,32,64]{1,4,3,2,0:T(8,128)} fusion(f32[4,32]{1,0:T(4,128)} %mul.308, bf16[2,128,4,32,64]{1,0,4,3,2:T(2,128)(2,1)S(1)} %copy-done.2, f32[4,32,2,128]{3,1,0,2:T(8,128)} %copy.35, f32[4,2,128,128]{3,2,0,1:T(8,128)S(1)} %convolution_bitcast_fusion, pred[128,128]{1,0:T(8,128)(4,1)} %iota_compare_fusion, ...), kind=kOutput, calls=%fused_computation.9 | convolution fusion | flops 3244294144 | bytes 13386240 | tf_op jit(solution)/shard_map/gjkts,ksgjp->ktgjp/dot_general | solution.py:72
  99.9 6.1 %slice_add_fusion = f32[1,128,4,32,64]{1,4,3,2,0:T(8,128)S(1)} fusion(f32[2,128,4,32,64]{1,4,3,2,0:T(8,128)} %bitcast_add_fusion, f32[4,32,64,128]{3,2,1,0:T(8,128)} %get-tuple-element.21, f32[128,4,32]{0,2,1:T(8,128)S(1)} %copy-done.11, bf16[2,128,4,128]{3,1,0,2:T(8,128)(2,1)S(1)} %bitcast.156), kind=kOutput, calls=%fused_computation.27 | convolution fusion | flops 1612709888 | bytes 12779520 | tf_op jit(solution)/shard_map/ktgn,kgjpn->ktgjp/dot_general | solution.py:78
  106.0 4.2 %pad_maximum_fusion = f32[2,128,4,32,64]{1,4,3,2,0:T(8,128)} fusion(f32[1,128,4,32,64]{1,4,3,2,0:T(8,128)S(1)} %slice_add_fusion, f32[1,128,4,32,64]{1,4,3,2,0:T(8,128)S(1)} %slice-done), kind=kLoop, calls=%fused_computation.7 | loop fusion | flops 2097152 | bytes 16777216 | tf_op jit(solution)/shard_map/concatenate | solution.py:80
  110.2 3.9 %collective-permute-done.3 = f32[3073,128]{1,0:T(8,128)} collective-permute-done((f32[3073,128]{1,0:T(8,128)S(1)}, f32[3073,128]{1,0:T(8,128)}, u32[]{:S(2)}, u32[]{:S(2)}) %collective-permute-start.3) | collective-permute-done | bytes 1573408 | tf_op jit(solution)/shard_map/ppermute | solution.py:165
  114.1 0.7 slice_add_fusion.6
  114.8 1.9 slice_add_fusion.2
  116.7 1.3 pad_maximum_fusion.3
  117.9 1.5 collective-permute-start.4
  120.1 1.4 mul.317
  121.5 34.5 %collective-permute-done.4 = f32[3073,128]{1,0:T(8,128)S(1)} collective-permute-done((f32[3073,128]{1,0:T(8,128)}, f32[3073,128]{1,0:T(8,128)S(1)}, u32[]{:S(2)}, u32[]{:S(2)}) %collective-permute-start.4) | collective-permute-done | bytes 1573408 | tf_op jit(solution)/shard_map/ppermute | solution.py:165
  156.1 1.2 copy-done.5
  157.3 1.3 slice_add_fusion.10
  158.5 1.9 multiply_add_fusion
  160.5 1.3 pad_maximum_fusion.4
  161.7 1.3 collective-permute-start.5
  163.2 0.7 exponential_bitcast_fusion.5
  164.2 69.3 %collective-permute-done.5 = f32[3073,128]{1,0:T(8,128)} collective-permute-done((f32[3073,128]{1,0:T(8,128)}, f32[3073,128]{1,0:T(8,128)}, u32[]{:S(2)}, u32[]{:S(2)}) %collective-permute-start.5) | collective-permute-done | bytes 1573408 | tf_op jit(solution)/shard_map/ppermute | solution.py:165
  233.5 3.3 fusion.33
  236.8 3.4 fusion.32
  240.7 1.9 collective-permute-start.6
  242.8 1.2 collective-permute-done.7
  244.0 8.5 %fusion.14 = f32[2,4,2,12,64,128]{5,4,0,3,2,1:T(8,128)} fusion(f32[2,4,2,12,128]{4,0,3,2,1:T(2,128)S(1)} %slice_bitcast_fusion.4, bf16[2,128,4,128,1,1]{3,1,0,5,4,2:T(8,128)(2,1)S(1)} %bitcast.157, f32[2,128,4,2,16,64]{1,5,4,3,2,0:T(8,128)} %bitcast.150, f32[4,1,12,64,128]{4,3,2,0,1:T(8,128)} %bitcast.39, f32[4,1,12,64,128]{4,3,2,0,1:T(8,128)S(1)} %get-tuple-element.39, ...), kind=kOutput, calls=%fused_computation.22 | convolution fusion | flops 1213464576 | bytes 16089089 | tf_op jit(solution)/shard_map/ktgn,ghrpn->kghrpt/dot_general | solution.py:116
  252.5 5.5 %collective-permute-done.6 = f32[1025,128]{1,0:T(8,128)} collective-permute-done((f32[1025,128]{1,0:T(8,128)S(1)}, f32[1025,128]{1,0:T(8,128)}, u32[]{:S(2)}, u32[]{:S(2)}) %collective-permute-start.6) | collective-permute-done | bytes 524832 | tf_op jit(solution)/shard_map/ppermute | solution.py:165
  258.7 1.2 slice_add_fusion.4
  259.9 0.8 copy-done.6
  260.7 0.9 pad_maximum_fusion.6
  261.6 1.3 collective-permute-start.9
  263.1 5.5 %dynamic-slice_bitcast_fusion.1 = (f32[4,2,12,64,128]{4,3,2,1,0:T(8,128)}, f32[4,2,12,64,128]{4,3,2,1,0:T(8,128)S(1)}) fusion(f32[2,4,2,12,64,128]{5,4,0,3,2,1:T(8,128)} %fusion.14, s32[]{:T(128)S(6)} %select_n.132, s32[]{:T(128)S(6)} %select_n.139), kind=kLoop, calls=%fused_computation.41 | loop fusion | bytes 12582920 | tf_op jit(solution)/shard_map/jit(dynamic_index_in_dim)/squeeze | solution.py:194
  268.6 1.5 collective-permute-start.8
  270.1 7.3 %collective-permute-done.9 = f32[1025,128]{1,0:T(8,128)} collective-permute-done((f32[1025,128]{1,0:T(8,128)}, f32[1025,128]{1,0:T(8,128)}, u32[]{:S(2)}, u32[]{:S(2)}) %collective-permute-start.9) | collective-permute-done | bytes 524832 | tf_op jit(solution)/shard_map/ppermute | solution.py:165
  278.0 1.2 multiply_add_fusion.1
  279.3 0.8 pad_maximum_fusion.7
  280.1 1.3 collective-permute-start.10
  282.4 23.8 %collective-permute-done.10 = f32[1025,128]{1,0:T(8,128)} collective-permute-done((f32[1025,128]{1,0:T(8,128)}, f32[1025,128]{1,0:T(8,128)}, u32[]{:S(2)}, u32[]{:S(2)}) %collective-permute-start.10) | collective-permute-done | bytes 524832 | tf_op jit(solution)/shard_map/ppermute | solution.py:165
  306.2 1.7 fusion.39
  307.9 1.4 fusion.38
  309.4 0.8 slice_bitcast_fusion.5
  310.1 1.1 collective-permute-done.11
  311.3 2.4 fusion.29
  313.7 1.5 dynamic-slice_bitcast_fusion.3
  315.2 1.5 collective-permute-start.12
  316.9 1.5 maximum_bitcast_fusion.1
  318.5 42.5 %collective-permute-done.12 = f32[4,2,4,64,128]{4,3,2,1,0:T(8,128)} collective-permute-done((f32[4,2,4,64,128]{4,3,2,1,0:T(8,128)}, f32[4,2,4,64,128]{4,3,2,1,0:T(8,128)}, u32[]{:S(2)}, u32[]{:S(2)}) %collective-permute-start.12) | collective-permute-done | bytes 1048608 | tf_op jit(solution)/shard_map/ppermute | solution.py:198
  361.0 2.5 maximum_bitcast_fusion
  363.5 4.5 %bitcast_select_fusion = f32[128,16384]{0,1:T(8,128)} fusion(f32[128,4,2,16,64]{0,4,3,2,1:T(8,128)S(1)} %maximum_bitcast_fusion.1, f32[128,4,2,16,64]{0,4,3,2,1:T(8,128)S(1)} %maximum_bitcast_fusion, pred[16384]{0:T(1024)(128)(4,1)S(1)} %broadcast_in_dim.96), kind=kLoop, calls=%fused_computation.8 | loop fusion | flops 2097152 | bytes 16793600 | tf_op jit(solution)/shard_map/jit(_where)/select_n | solution.py:145
  368.0 9.0 %copy.45 = f32[128,16384]{1,0:T(8,128)} copy(f32[128,16384]{0,1:T(8,128)} %bitcast_select_fusion) | data formatting | bytes 16777216 | tf_op jit(solution)/shard_map/jit(_where)/select_n | solution.py:145
  (112 shorter events, 10.3 us)
Async XLA Ops:
  0.0 7.2 %copy-start.12 = (bf16[4,4,2304]{2,1,0:T(4,128)(2,1)S(1)}, bf16[4,4,2304]{2,1,0:T(4,128)(2,1)}, u32[]{:S(2)}) copy-start(bf16[4,4,2304]{2,1,0:T(4,128)(2,1)} %param.9) | copy-start | bytes 221188
  0.0 7.2 %copy-start.20 = (f32[128]{0:T(128)S(1)}, f32[128]{0:T(128)}, u32[]{:S(2)}) copy-start(f32[128]{0:T(128)} %param.12) | copy-start | bytes 1540
  0.0 7.2 %copy-start.17 = (f32[128]{0:T(128)S(1)}, f32[128]{0:T(128)}, u32[]{:S(2)}) copy-start(f32[128]{0:T(128)} %param.11) | copy-start | bytes 1540
  0.0 7.2 %copy-start.13 = (bf16[128,256]{1,0:T(8,128)(2,1)S(1)}, bf16[128,256]{1,0:T(8,128)(2,1)}, u32[]{:S(2)}) copy-start(bf16[128,256]{1,0:T(8,128)(2,1)} %param.8) | copy-start | bytes 196612
  0.0 10.3 %copy-start.15 = (bf16[4,2304]{1,0:T(4,128)(2,1)S(1)}, bf16[4,2304]{1,0:T(4,128)(2,1)}, u32[]{:S(2)}) copy-start(bf16[4,2304]{1,0:T(4,128)(2,1)} %param.10) | copy-start | bytes 55300
  3.0 2.2 copy-start.1
  5.3 6.6 %collective-permute-start.1 = (bf16[3,4,2304]{2,0,1:T(4,128)(2,1)S(1)}, bf16[3,4,2304]{2,0,1:T(4,128)(2,1)S(1)}, u32[]{:S(2)}, u32[]{:S(2)}) collective-permute-start(bf16[3,4,2304]{2,0,1:T(4,128)(2,1)S(1)} %slice.257), channel_id=1, source_target_pairs={{0,2},{2,4},{4,6},{6,8},{8,10},{10,12},{12,14},{14,16},{16,18},{18... | collective-permute-start | bytes 165896 | tf_op jit(solution)/shard_map/ppermute | solution.py:15
  28.2 23.7 %copy-start.8 = (bf16[256,4,128]{2,0,1:T(8,128)(2,1)}, bf16[256,4,128]{2,0,1:T(8,128)(2,1)S(1)}, u32[]{:S(2)}) copy-start(bf16[256,4,128]{2,0,1:T(8,128)(2,1)S(1)} %get-tuple-element.34) | copy-start | bytes 786436
  61.7 2.1 copy-start
  61.7 6.0 %copy-start.18 = (f32[128]{0:T(128)S(1)}, f32[128]{0:T(128)}, u32[]{:S(2)}) copy-start(f32[128]{0:T(128)} %param.13) | copy-start | bytes 1540
  65.3 4.6 %collective-permute-start.2 = (f32[4,16,64,128]{3,2,1,0:T(8,128)}, f32[4,16,64,128]{3,2,1,0:T(8,128)S(1)}, u32[]{:S(2)}, u32[]{:S(2)}) collective-permute-start(f32[4,16,64,128]{3,2,1,0:T(8,128)} %constant_dynamic-slice_fusion.1), channel_id=1, source_target_pairs={{0,2},{2,0},{1,3},{3,1},{4,6},{6,4},{5,7},{7,5},{8,10},{10,8},{9,1... | collective-permute-start | bytes 6291464 | tf_op jit(solution)/shard_map/ppermute | solution.py:91
  65.6 4.1 %collective-permute-start = (f32[4,32]{1,0:T(4,128)S(1)}, f32[4,32]{1,0:T(4,128)S(1)}, u32[]{:S(2)}, u32[]{:S(2)}) collective-permute-start(f32[4,32]{1,0:T(4,128)S(1)} %get-tuple-element.46), channel_id=1, source_target_pairs={{0,2},{2,0},{1,3},{3,1},{4,6},{6,4},{5,7},{7,5},{8,10},{10,8},{9,1... | collective-permute-start | bytes 1544 | tf_op jit(solution)/shard_map/ppermute | solution.py:86
  69.8 4.3 %copy-start.4 = (f32[4,16,64,128]{3,2,1,0:T(8,128)}, f32[4,16,64,128]{3,2,1,0:T(8,128)S(1)}, u32[]{:S(2)}) copy-start(f32[4,16,64,128]{3,2,1,0:T(8,128)S(1)} %collective-permute-done.2) | copy-start | bytes 6291460
  72.6 1.4 copy-start.3
  73.9 3.3 copy-start.9
  73.9 3.6 copy-start.2
  74.2 39.8 %collective-permute-start.3 = (f32[3073,128]{1,0:T(8,128)S(1)}, f32[3073,128]{1,0:T(8,128)}, u32[]{:S(2)}, u32[]{:S(2)}) collective-permute-start(f32[3073,128]{1,0:T(8,128)S(1)} %pad_maximum_fusion.2), channel_id=1, source_target_pairs={{0,4},{4,8},{8,12},{12,16},{16,20},{20,24},{24,28},{1,5},{5,9},{9,... | collective-permute-start | bytes 4720136 | tf_op jit(solution)/shard_map/ppermute | solution.py:165
  99.0 0.8 copy-start.11
  99.9 6.1 %slice-start = ((f32[2,128,4,32,64]{1,4,3,2,0:T(8,128)}), f32[1,128,4,32,64]{1,4,3,2,0:T(8,128)S(1)}, s32[]{:S(2)}) async-start(f32[2,128,4,32,64]{1,4,3,2,0:T(8,128)} %bitcast_add_fusion), calls=%async_computation | async-start | bytes 8388608 | tf_op jit(solution)/shard_map/slice | solution.py:80
  106.0 8.8 %copy-start.14 = (f32[3072]{0:T(1024)S(1)}, f32[3072]{0:T(1024)}, u32[]{:S(2)}) copy-start(f32[3072]{0:T(1024)} %mul.302) | copy-start | bytes 36868
  114.8 4.7 %copy-start.16 = (f32[1,128]{1,0:T(1,128)}, f32[1,128]{1,0:T(1,128)S(1)}, u32[]{:S(2)}) copy-start(f32[1,128]{1,0:T(1,128)S(1)} %slice_add_fusion.6) | copy-start | bytes 1540
  117.9 38.1 %collective-permute-start.4 = (f32[3073,128]{1,0:T(8,128)}, f32[3073,128]{1,0:T(8,128)S(1)}, u32[]{:S(2)}, u32[]{:S(2)}) collective-permute-start(f32[3073,128]{1,0:T(8,128)} %pad_maximum_fusion.3), channel_id=1, source_target_pairs={{0,8},{4,12},{8,16},{12,20},{16,24},{20,28},{1,9},{5,13},{9,17},{1... | collective-permute-start | bytes 4720136 | tf_op jit(solution)/shard_map/ppermute | solution.py:165
  156.1 1.2 copy-start.5
  158.5 4.7 %slice-start.1 = ((f32[4,16,64,128]{3,2,1,0:T(8,128)}), f32[4,4,64,128]{3,2,1,0:T(8,128)S(1)}, s32[]{:S(2)}) async-start(f32[4,16,64,128]{3,2,1,0:T(8,128)} %copy-done.3), calls=%async_computation.1 | async-start | bytes 1048576 | tf_op jit(solution)/shard_map/slice | solution.py:133
  158.5 5.5 %copy-start.19 = (f32[1,128]{1,0:T(1,128)S(1)}, f32[1,128]{1,0:T(1,128)}, u32[]{:S(2)}) copy-start(f32[1,128]{1,0:T(1,128)} %get-tuple-element.37) | copy-start | bytes 1540
  161.7 71.8 %collective-permute-start.5 = (f32[3073,128]{1,0:T(8,128)}, f32[3073,128]{1,0:T(8,128)}, u32[]{:S(2)}, u32[]{:S(2)}) collective-permute-start(f32[3073,128]{1,0:T(8,128)} %pad_maximum_fusion.4), channel_id=1, source_target_pairs={{0,16},{4,20},{8,24},{12,28},{1,17},{5,21},{9,25},{13,29},{2,18},{... | collective-permute-start | bytes 4720136 | tf_op jit(solution)/shard_map/ppermute | solution.py:165
  240.2 3.8 collective-permute-start.7
  240.7 11.8 %copy-start.10 = (f32[4,2,16,2,128]{4,3,2,1,0:T(2,128)}, f32[4,2,16,2,128]{4,3,2,1,0:T(2,128)S(1)}, u32[]{:S(2)}) copy-start(f32[4,2,16,2,128]{4,3,2,1,0:T(2,128)S(1)} %fusion.42) | copy-start | bytes 393220
  240.7 17.3 %collective-permute-start.6 = (f32[1025,128]{1,0:T(8,128)S(1)}, f32[1025,128]{1,0:T(8,128)}, u32[]{:S(2)}, u32[]{:S(2)}) collective-permute-start(f32[1025,128]{1,0:T(8,128)S(1)} %pad_maximum_fusion.5), channel_id=1, source_target_pairs={{0,4},{4,8},{8,12},{12,16},{16,20},{20,24},{24,28},{1,5},{5,9},{9,... | collective-permute-start | bytes 1574408 | tf_op jit(solution)/shard_map/ppermute | solution.py:165
  259.9 0.8 copy-start.6
  261.6 15.8 %collective-permute-start.9 = (f32[1025,128]{1,0:T(8,128)}, f32[1025,128]{1,0:T(8,128)}, u32[]{:S(2)}, u32[]{:S(2)}) collective-permute-start(f32[1025,128]{1,0:T(8,128)} %pad_maximum_fusion.6), channel_id=1, source_target_pairs={{0,8},{4,12},{8,16},{12,20},{16,24},{20,28},{1,9},{5,13},{9,17},{1... | collective-permute-start | bytes 1574408 | tf_op jit(solution)/shard_map/ppermute | solution.py:165
  263.1 15.0 %copy-start.7 = (f32[1024,128]{1,0:T(8,128)S(1)}, f32[1024,128]{1,0:T(8,128)}, u32[]{:S(2)}) copy-start(f32[1024,128]{1,0:T(8,128)} %copy-done.6) | copy-start | bytes 1572868
  268.6 92.4 %collective-permute-start.8 = (f32[4,2,12,64,128]{4,3,2,1,0:T(8,128)}, f32[4,2,12,64,128]{4,3,2,1,0:T(8,128)}, u32[]{:S(2)}, u32[]{:S(2)}) collective-permute-start(f32[4,2,12,64,128]{4,3,2,1,0:T(8,128)} %get-tuple-element.31), channel_id=1, source_target_pairs={{0,1},{1,0},{2,3},{3,2},{4,5},{5,4},{6,7},{7,6},{8,9},{9,8},{10,11... | collective-permute-start | bytes 9437192 | tf_op jit(solution)/shard_map/ppermute | solution.py:198
  280.1 26.1 %collective-permute-start.10 = (f32[1025,128]{1,0:T(8,128)}, f32[1025,128]{1,0:T(8,128)}, u32[]{:S(2)}, u32[]{:S(2)}) collective-permute-start(f32[1025,128]{1,0:T(8,128)} %pad_maximum_fusion.7), channel_id=1, source_target_pairs={{0,16},{4,20},{8,24},{12,28},{1,17},{5,21},{9,25},{13,29},{2,18},{... | collective-permute-start | bytes 1574408 | tf_op jit(solution)/shard_map/ppermute | solution.py:165
  309.3 2.0 collective-permute-start.11
  315.2 45.8 %collective-permute-start.12 = (f32[4,2,4,64,128]{4,3,2,1,0:T(8,128)}, f32[4,2,4,64,128]{4,3,2,1,0:T(8,128)}, u32[]{:S(2)}, u32[]{:S(2)}) collective-permute-start(f32[4,2,4,64,128]{4,3,2,1,0:T(8,128)} %get-tuple-element.35), channel_id=1, source_target_pairs={{0,1},{1,0},{2,3},{3,2},{4,5},{5,4},{6,7},{7,6},{8,9},{9,8},{10,11... | collective-permute-start | bytes 3145736 | tf_op jit(solution)/shard_map/ppermute | solution.py:198

commit v2 on v1

--- a/solution.py
+++ b/solution.py
@@ -47,7 +47,7 @@
     values32 = values
     weights = jnp.exp(chunk_log[..., None] - cum) * steps
     weighted = values32 * jnp.transpose(weights, (2, 3, 0, 1))[..., None]
-    chunk_states = jnp.einsum("ksgn,ksgjp->kgjpn", b_part.astype(f32), weighted, precision=exact)
+    chunk_states = jnp.einsum("ksgn,ksgjp->kgjpn", b_part.astype(f32), weighted, precision=lax.Precision.HIGH)
 
     running = jnp.zeros_like(chunk_states[0])
     local_list = []
@@ -113,10 +113,10 @@
         )
         base = intra_out.reshape(nck, chunk, group_count, 2, half, HEAD_DIM)[:, :, :, :, part]
         if by_chunk:
-            carried = jnp.einsum("ktgn,ghrpn->kghrpt", c32, incoming, precision=lax.Precision.HIGH)
+            carried = jnp.einsum("ktgn,ghrpn->kghrpt", c32, incoming, precision=exact)
             scale = jnp.transpose(grow[:, :, part], (3, 0, 1, 2, 4))[:, :, :, :, None, :]
             return jnp.transpose(base, (0, 2, 3, 4, 5, 1)) + scale * carried
-        carried = jnp.einsum("ktgn,ghrpn->ktghrp", c32, incoming, precision=lax.Precision.HIGH)
+        carried = jnp.einsum("ktgn,ghrpn->ktghrp", c32, incoming, precision=exact)
         scale = jnp.transpose(grow[:, :, part], (3, 4, 0, 1, 2))[..., None]
         return (base + scale * carried).reshape(row_count, -1)
 

time: 382 us -> 380 us (level)
  no operation moved by 1% of the time
where the time goes in v2:
time: 380 us; the launch traced here: 376 us
  waiting for transfers between devices  191 us (50%)
  other arithmetic  69.6 us (18%)
  local copies, waits for them, and re-layouts  53.2 us (14%)
  matrix products  45.9 us (12%)
  starting transfers between devices  15.8 us (4%)
    ppermute x6, waiting for transfers between devices, shifted(): lax.ppermute(value, 'fh', [(d, d + step) for d in range(count - step)])  143 us
    ppermute x2, waiting for transfers between devices, exchange_chunks(): lax.ppermute(sent, 'tp', [(d, (d + shift) % tp_count) for d in range(tp_c...  42.2 us
    dot_general x1, matrix products, intra(): output = jnp.einsum('gjkts,ksgjp->ktgjp', mixing, values32, precision=exact)  21.5 us
    convert_element_type x1, other arithmetic, convolve(): return jax.nn.silu(summed).astype(jnp.bfloat16)  13.7 us
    dot_general x2, matrix products, finish(): carried = jnp.einsum('ktgn,ghrpn->kghrpt', c32, incoming, precision=exact)  12 us
    add x6, other arithmetic, combine(): body = scale * got[:-log_rows] + cur[:-log_rows]  11.3 us
    unnamed x44, local copies, waits for them, and re-layouts  10.8 us
    mul x1, other arithmetic, shards(): weighted = values32 * jnp.transpose(weights, (2, 3, 0, 1))[..., None]  10.5 us
  transfers between devices with their start and end apart: 13, of which 11 were waited for; matrix products, arithmetic and copies ran while one was open for 19% of the time, Pallas kernels for 0%

profile of v2, /device:TPU:24, one launch (start us, length us, event | category | flops | bytes accessed | tf_op | source)
XLA Modules:
  0.0 375.6 jit_solution(17883699796157496960)
XLA Ops:
  0.0 3.0 copy.24
  3.0 2.2 copy-done.1
  5.3 1.9 collective-permute-start.1
  7.5 2.3 reduce_window_sum.24
  10.5 1.3 collective-permute-done.1
  11.8 13.7 %multiply_convert_fusion = bf16[256,4,2304]{2,0,1:T(8,128)(2,1)S(1)} fusion(bf16[256,4,2304]{2,0,1:T(8,128)(2,1)} %copy-done.1, bf16[3,4,2304]{2,0,1:T(4,128)(2,1)S(1)} %collective-permute-done.1, f32[4,2304]{1,0:T(4,128)S(1)} %get-tuple-element.49, f32[4,2304]{1,0:T(4,128)S(1)} %get-tuple-element.50, f32[4,2304]{1,0:T(4,128)S(1)} %get-tuple-element.48, ...), kind=kLoop, calls=%fused_computation.6 | loop fusion | flops 61341696 | bytes 9676800 | tf_op jit(solution)/shard_map/convert_element_type | solution.py:22
  25.5 2.6 slice.262
  28.2 6.3 %copy.27 = bf16[256,4,2048]{0,2,1:T(8,128)(2,1)} copy(bf16[256,4,2048]{2,0,1:T(8,128)(2,1)} %slice.262) | data formatting | bytes 8388608 | tf_op jit(solution)/shard_map/slice | solution.py:36
  34.5 6.9 %reshape.130 = bf16[2,128,4,32,64]{1,0,4,3,2:T(2,128)(2,1)} reshape(bf16[256,4,2048]{0,2,1:T(8,128)(2,1)} %copy.27) | data formatting | bytes 8388608 | tf_op jit(solution)/shard_map/reshape | solution.py:36
  41.4 10.5 %convert_multiply_fusion = f32[2,128,4,32,64]{1,0,4,3,2:T(2,128)} fusion(bf16[2,128,4,32,64]{1,0,4,3,2:T(2,128)(2,1)} %reshape.130, f32[2,128,4,32]{1,0,3,2:T(2,128)S(1)} %copy.30), kind=kLoop, calls=%fused_computation.17 | loop fusion | flops 4194304 | bytes 12713984 | tf_op jit(solution)/shard_map/mul | solution.py:49
  52.0 5.9 %fusion.6 = f32[2,4,32,64,128]{4,3,2,1,0:T(8,128)S(1)} fusion(f32[2,128,4,32,64]{1,0,4,3,2:T(2,128)} %convert_multiply_fusion, bf16[2,128,4,128,1]{3,1,0,2,4:T(8,128)(2,1)S(1)} %bitcast.160), kind=kOutput, calls=%fused_computation.10 | convolution fusion | flops 1610612736 | bytes 17039360 | tf_op jit(solution)/shard_map/ksgn,ksgjp->kgjpn/dot_general | solution.py:50
  57.9 2.4 fusion.17
  60.3 2.1 copy-done
  62.4 1.5 constant_dynamic-slice_fusion.1
  66.9 1.3 collective-permute-done
  68.4 2.7 select_add_fusion
  71.1 1.4 copy-done.3
  72.8 2.9 collective-permute-start.3
  76.1 21.5 %bitcast_add_fusion = f32[2,128,4,32,64]{1,4,3,2,0:T(8,128)} fusion(f32[4,32]{1,0:T(4,128)} %mul.308, bf16[2,128,4,32,64]{1,0,4,3,2:T(2,128)(2,1)S(1)} %copy-done.2, f32[4,32,2,128]{3,1,0,2:T(8,128)} %copy.35, f32[4,2,128,128]{3,2,0,1:T(8,128)S(1)} %convolution_bitcast_fusion, pred[128,128]{1,0:T(8,128)(4,1)} %iota_compare_fusion, ...), kind=kOutput, calls=%fused_computation.9 | convolution fusion | flops 3244294144 | bytes 13386240 | tf_op jit(solution)/shard_map/gjkts,ksgjp->ktgjp/dot_general | solution.py:72
  98.4 6.1 %slice_add_fusion = f32[1,128,4,32,64]{1,4,3,2,0:T(8,128)S(1)} fusion(f32[2,128,4,32,64]{1,4,3,2,0:T(8,128)} %bitcast_add_fusion, f32[4,32,64,128]{3,2,1,0:T(8,128)} %get-tuple-element.21, f32[128,4,32]{0,2,1:T(8,128)S(1)} %copy-done.11, bf16[2,128,4,128]{3,1,0,2:T(8,128)(2,1)S(1)} %bitcast.156), kind=kOutput, calls=%fused_computation.27 | convolution fusion | flops 1612709888 | bytes 12779520 | tf_op jit(solution)/shard_map/ktgn,kgjpn->ktgjp/dot_general | solution.py:78
  104.6 4.2 %pad_maximum_fusion = f32[2,128,4,32,64]{1,4,3,2,0:T(8,128)} fusion(f32[1,128,4,32,64]{1,4,3,2,0:T(8,128)S(1)} %slice_add_fusion, f32[1,128,4,32,64]{1,4,3,2,0:T(8,128)S(1)} %slice-done), kind=kLoop, calls=%fused_computation.7 | loop fusion | flops 2097152 | bytes 16777216 | tf_op jit(solution)/shard_map/concatenate | solution.py:80
  108.8 3.9 %collective-permute-done.3 = f32[3073,128]{1,0:T(8,128)} collective-permute-done((f32[3073,128]{1,0:T(8,128)S(1)}, f32[3073,128]{1,0:T(8,128)}, u32[]{:S(2)}, u32[]{:S(2)}) %collective-permute-start.3) | collective-permute-done | bytes 1573408 | tf_op jit(solution)/shard_map/ppermute | solution.py:165
  112.6 0.7 slice_add_fusion.6
  113.3 1.9 slice_add_fusion.2
  115.2 1.3 pad_maximum_fusion.3
  116.5 1.5 collective-permute-start.4
  118.7 1.4 mul.317
  120.1 34.5 %collective-permute-done.4 = f32[3073,128]{1,0:T(8,128)S(1)} collective-permute-done((f32[3073,128]{1,0:T(8,128)}, f32[3073,128]{1,0:T(8,128)S(1)}, u32[]{:S(2)}, u32[]{:S(2)}) %collective-permute-start.4) | collective-permute-done | bytes 1573408 | tf_op jit(solution)/shard_map/ppermute | solution.py:165
  154.6 1.2 copy-done.5
  155.8 1.3 slice_add_fusion.10
  157.1 1.9 multiply_add_fusion
  159.0 1.3 pad_maximum_fusion.4
  160.3 1.3 collective-permute-start.5
  161.8 0.7 exponential_bitcast_fusion.5
  162.8 69.3 %collective-permute-done.5 = f32[3073,128]{1,0:T(8,128)} collective-permute-done((f32[3073,128]{1,0:T(8,128)}, f32[3073,128]{1,0:T(8,128)}, u32[]{:S(2)}, u32[]{:S(2)}) %collective-permute-start.5) | collective-permute-done | bytes 1573408 | tf_op jit(solution)/shard_map/ppermute | solution.py:165
  232.0 3.3 fusion.33
  235.4 3.4 fusion.32
  239.3 1.9 collective-permute-start.6
  241.4 1.2 collective-permute-done.7
  242.6 9.3 %fusion.14 = f32[2,4,2,12,64,128]{5,4,0,3,2,1:T(8,128)} fusion(f32[2,4,2,12,128]{4,0,3,2,1:T(2,128)S(1)} %slice_bitcast_fusion.4, bf16[2,128,4,128,1,1]{3,1,0,5,4,2:T(8,128)(2,1)S(1)} %bitcast.157, f32[2,128,4,2,16,64]{1,5,4,3,2,0:T(8,128)} %bitcast.150, f32[4,1,12,64,128]{4,3,2,0,1:T(8,128)} %bitcast.39, f32[4,1,12,64,128]{4,3,2,0,1:T(8,128)S(1)} %get-tuple-element.39, ...), kind=kOutput, calls=%fused_computation.22 | convolution fusion | flops 2421424128 | bytes 16089089 | tf_op jit(solution)/shard_map/ktgn,ghrpn->kghrpt/dot_general | solution.py:116
  251.9 4.7 %collective-permute-done.6 = f32[1025,128]{1,0:T(8,128)} collective-permute-done((f32[1025,128]{1,0:T(8,128)S(1)}, f32[1025,128]{1,0:T(8,128)}, u32[]{:S(2)}, u32[]{:S(2)}) %collective-permute-start.6) | collective-permute-done | bytes 524832 | tf_op jit(solution)/shard_map/ppermute | solution.py:165
  257.3 1.2 slice_add_fusion.4
  258.5 0.8 copy-done.6
  259.3 0.9 pad_maximum_fusion.6
  260.2 1.3 collective-permute-start.9
  261.6 5.5 %dynamic-slice_bitcast_fusion.1 = (f32[4,2,12,64,128]{4,3,2,1,0:T(8,128)}, f32[4,2,12,64,128]{4,3,2,1,0:T(8,128)S(1)}) fusion(f32[2,4,2,12,64,128]{5,4,0,3,2,1:T(8,128)} %fusion.14, s32[]{:T(128)S(6)} %select_n.132, s32[]{:T(128)S(6)} %select_n.139), kind=kLoop, calls=%fused_computation.41 | loop fusion | bytes 12582920 | tf_op jit(solution)/shard_map/jit(dynamic_index_in_dim)/squeeze | solution.py:194
  267.1 1.5 collective-permute-start.8
  268.7 7.3 %collective-permute-done.9 = f32[1025,128]{1,0:T(8,128)} collective-permute-done((f32[1025,128]{1,0:T(8,128)}, f32[1025,128]{1,0:T(8,128)}, u32[]{:S(2)}, u32[]{:S(2)}) %collective-permute-start.9) | collective-permute-done | bytes 524832 | tf_op jit(solution)/shard_map/ppermute | solution.py:165
  276.6 1.2 multiply_add_fusion.1
  277.8 0.8 pad_maximum_fusion.7
  278.7 1.3 collective-permute-start.10
  281.0 23.8 %collective-permute-done.10 = f32[1025,128]{1,0:T(8,128)} collective-permute-done((f32[1025,128]{1,0:T(8,128)}, f32[1025,128]{1,0:T(8,128)}, u32[]{:S(2)}, u32[]{:S(2)}) %collective-permute-start.10) | collective-permute-done | bytes 524832 | tf_op jit(solution)/shard_map/ppermute | solution.py:165
  304.8 1.7 fusion.39
  306.5 1.4 fusion.38
  307.9 0.8 slice_bitcast_fusion.5
  308.7 1.1 collective-permute-done.11
  309.8 2.7 fusion.29
  312.6 1.5 dynamic-slice_bitcast_fusion.3
  314.1 1.5 collective-permute-start.12
  315.8 1.5 maximum_bitcast_fusion.1
  317.3 42.2 %collective-permute-done.12 = f32[4,2,4,64,128]{4,3,2,1,0:T(8,128)} collective-permute-done((f32[4,2,4,64,128]{4,3,2,1,0:T(8,128)}, f32[4,2,4,64,128]{4,3,2,1,0:T(8,128)}, u32[]{:S(2)}, u32[]{:S(2)}) %collective-permute-start.12) | collective-permute-done | bytes 1048608 | tf_op jit(solution)/shard_map/ppermute | solution.py:198
  359.6 2.5 maximum_bitcast_fusion
  362.1 4.5 %bitcast_select_fusion = f32[128,16384]{0,1:T(8,128)} fusion(f32[128,4,2,16,64]{0,4,3,2,1:T(8,128)S(1)} %maximum_bitcast_fusion.1, f32[128,4,2,16,64]{0,4,3,2,1:T(8,128)S(1)} %maximum_bitcast_fusion, pred[16384]{0:T(1024)(128)(4,1)S(1)} %broadcast_in_dim.96), kind=kLoop, calls=%fused_computation.8 | loop fusion | flops 2097152 | bytes 16793600 | tf_op jit(solution)/shard_map/jit(_where)/select_n | solution.py:145
  366.6 9.0 %copy.45 = f32[128,16384]{1,0:T(8,128)} copy(f32[128,16384]{0,1:T(8,128)} %bitcast_select_fusion) | data formatting | bytes 16777216 | tf_op jit(solution)/shard_map/jit(_where)/select_n | solution.py:145
  (112 shorter events, 10.3 us)
Async XLA Ops:
  0.0 7.2 %copy-start.12 = (bf16[4,4,2304]{2,1,0:T(4,128)(2,1)S(1)}, bf16[4,4,2304]{2,1,0:T(4,128)(2,1)}, u32[]{:S(2)}) copy-start(bf16[4,4,2304]{2,1,0:T(4,128)(2,1)} %param.9) | copy-start | bytes 221188
  0.0 7.2 %copy-start.20 = (f32[128]{0:T(128)S(1)}, f32[128]{0:T(128)}, u32[]{:S(2)}) copy-start(f32[128]{0:T(128)} %param.12) | copy-start | bytes 1540
  0.0 7.2 %copy-start.17 = (f32[128]{0:T(128)S(1)}, f32[128]{0:T(128)}, u32[]{:S(2)}) copy-start(f32[128]{0:T(128)} %param.11) | copy-start | bytes 1540
  0.0 7.2 %copy-start.13 = (bf16[128,256]{1,0:T(8,128)(2,1)S(1)}, bf16[128,256]{1,0:T(8,128)(2,1)}, u32[]{:S(2)}) copy-start(bf16[128,256]{1,0:T(8,128)(2,1)} %param.8) | copy-start | bytes 196612
  0.0 10.3 %copy-start.15 = (bf16[4,2304]{1,0:T(4,128)(2,1)S(1)}, bf16[4,2304]{1,0:T(4,128)(2,1)}, u32[]{:S(2)}) copy-start(bf16[4,2304]{1,0:T(4,128)(2,1)} %param.10) | copy-start | bytes 55300
  3.0 2.2 copy-start.1
  5.3 6.6 %collective-permute-start.1 = (bf16[3,4,2304]{2,0,1:T(4,128)(2,1)S(1)}, bf16[3,4,2304]{2,0,1:T(4,128)(2,1)S(1)}, u32[]{:S(2)}, u32[]{:S(2)}) collective-permute-start(bf16[3,4,2304]{2,0,1:T(4,128)(2,1)S(1)} %slice.257), channel_id=1, source_target_pairs={{0,2},{2,4},{4,6},{6,8},{8,10},{10,12},{12,14},{14,16},{16,18},{18... | collective-permute-start | bytes 165896 | tf_op jit(solution)/shard_map/ppermute | solution.py:15
  28.2 23.7 %copy-start.8 = (bf16[256,4,128]{2,0,1:T(8,128)(2,1)}, bf16[256,4,128]{2,0,1:T(8,128)(2,1)S(1)}, u32[]{:S(2)}) copy-start(bf16[256,4,128]{2,0,1:T(8,128)(2,1)S(1)} %get-tuple-element.34) | copy-start | bytes 786436
  60.3 2.1 copy-start
  60.3 6.0 %copy-start.18 = (f32[128]{0:T(128)S(1)}, f32[128]{0:T(128)}, u32[]{:S(2)}) copy-start(f32[128]{0:T(128)} %param.13) | copy-start | bytes 1540
  63.8 4.6 %collective-permute-start.2 = (f32[4,16,64,128]{3,2,1,0:T(8,128)}, f32[4,16,64,128]{3,2,1,0:T(8,128)S(1)}, u32[]{:S(2)}, u32[]{:S(2)}) collective-permute-start(f32[4,16,64,128]{3,2,1,0:T(8,128)} %constant_dynamic-slice_fusion.1), channel_id=1, source_target_pairs={{0,2},{2,0},{1,3},{3,1},{4,6},{6,4},{5,7},{7,5},{8,10},{10,8},{9,1... | collective-permute-start | bytes 6291464 | tf_op jit(solution)/shard_map/ppermute | solution.py:91
  64.1 4.1 %collective-permute-start = (f32[4,32]{1,0:T(4,128)S(1)}, f32[4,32]{1,0:T(4,128)S(1)}, u32[]{:S(2)}, u32[]{:S(2)}) collective-permute-start(f32[4,32]{1,0:T(4,128)S(1)} %get-tuple-element.46), channel_id=1, source_target_pairs={{0,2},{2,0},{1,3},{3,1},{4,6},{6,4},{5,7},{7,5},{8,10},{10,8},{9,1... | collective-permute-start | bytes 1544 | tf_op jit(solution)/shard_map/ppermute | solution.py:86
  68.4 4.3 %copy-start.4 = (f32[4,16,64,128]{3,2,1,0:T(8,128)}, f32[4,16,64,128]{3,2,1,0:T(8,128)S(1)}, u32[]{:S(2)}) copy-start(f32[4,16,64,128]{3,2,1,0:T(8,128)S(1)} %collective-permute-done.2) | copy-start | bytes 6291460
  71.1 1.4 copy-start.3
  72.5 3.3 copy-start.9
  72.5 3.6 copy-start.2
  72.8 39.8 %collective-permute-start.3 = (f32[3073,128]{1,0:T(8,128)S(1)}, f32[3073,128]{1,0:T(8,128)}, u32[]{:S(2)}, u32[]{:S(2)}) collective-permute-start(f32[3073,128]{1,0:T(8,128)S(1)} %pad_maximum_fusion.2), channel_id=1, source_target_pairs={{0,4},{4,8},{8,12},{12,16},{16,20},{20,24},{24,28},{1,5},{5,9},{9,... | collective-permute-start | bytes 4720136 | tf_op jit(solution)/shard_map/ppermute | solution.py:165
  97.6 0.8 copy-start.11
  98.4 6.1 %slice-start = ((f32[2,128,4,32,64]{1,4,3,2,0:T(8,128)}), f32[1,128,4,32,64]{1,4,3,2,0:T(8,128)S(1)}, s32[]{:S(2)}) async-start(f32[2,128,4,32,64]{1,4,3,2,0:T(8,128)} %bitcast_add_fusion), calls=%async_computation | async-start | bytes 8388608 | tf_op jit(solution)/shard_map/slice | solution.py:80
  104.5 8.8 %copy-start.14 = (f32[3072]{0:T(1024)S(1)}, f32[3072]{0:T(1024)}, u32[]{:S(2)}) copy-start(f32[3072]{0:T(1024)} %mul.302) | copy-start | bytes 36868
  113.3 4.7 %copy-start.16 = (f32[1,128]{1,0:T(1,128)}, f32[1,128]{1,0:T(1,128)S(1)}, u32[]{:S(2)}) copy-start(f32[1,128]{1,0:T(1,128)S(1)} %slice_add_fusion.6) | copy-start | bytes 1540
  116.5 38.1 %collective-permute-start.4 = (f32[3073,128]{1,0:T(8,128)}, f32[3073,128]{1,0:T(8,128)S(1)}, u32[]{:S(2)}, u32[]{:S(2)}) collective-permute-start(f32[3073,128]{1,0:T(8,128)} %pad_maximum_fusion.3), channel_id=1, source_target_pairs={{0,8},{4,12},{8,16},{12,20},{16,24},{20,28},{1,9},{5,13},{9,17},{1... | collective-permute-start | bytes 4720136 | tf_op jit(solution)/shard_map/ppermute | solution.py:165
  154.6 1.2 copy-start.5
  157.1 4.7 %slice-start.1 = ((f32[4,16,64,128]{3,2,1,0:T(8,128)}), f32[4,4,64,128]{3,2,1,0:T(8,128)S(1)}, s32[]{:S(2)}) async-start(f32[4,16,64,128]{3,2,1,0:T(8,128)} %copy-done.3), calls=%async_computation.1 | async-start | bytes 1048576 | tf_op jit(solution)/shard_map/slice | solution.py:133
  157.1 5.5 %copy-start.19 = (f32[1,128]{1,0:T(1,128)S(1)}, f32[1,128]{1,0:T(1,128)}, u32[]{:S(2)}) copy-start(f32[1,128]{1,0:T(1,128)} %get-tuple-element.37) | copy-start | bytes 1540
  160.3 71.8 %collective-permute-start.5 = (f32[3073,128]{1,0:T(8,128)}, f32[3073,128]{1,0:T(8,128)}, u32[]{:S(2)}, u32[]{:S(2)}) collective-permute-start(f32[3073,128]{1,0:T(8,128)} %pad_maximum_fusion.4), channel_id=1, source_target_pairs={{0,16},{4,20},{8,24},{12,28},{1,17},{5,21},{9,25},{13,29},{2,18},{... | collective-permute-start | bytes 4720136 | tf_op jit(solution)/shard_map/ppermute | solution.py:165
  238.8 3.8 collective-permute-start.7
  239.2 12.6 %copy-start.10 = (f32[4,2,16,2,128]{4,3,2,1,0:T(2,128)}, f32[4,2,16,2,128]{4,3,2,1,0:T(2,128)S(1)}, u32[]{:S(2)}) copy-start(f32[4,2,16,2,128]{4,3,2,1,0:T(2,128)S(1)} %fusion.42) | copy-start | bytes 393220
  239.3 17.3 %collective-permute-start.6 = (f32[1025,128]{1,0:T(8,128)S(1)}, f32[1025,128]{1,0:T(8,128)}, u32[]{:S(2)}, u32[]{:S(2)}) collective-permute-start(f32[1025,128]{1,0:T(8,128)S(1)} %pad_maximum_fusion.5), channel_id=1, source_target_pairs={{0,4},{4,8},{8,12},{12,16},{16,20},{20,24},{24,28},{1,5},{5,9},{9,... | collective-permute-start | bytes 1574408 | tf_op jit(solution)/shard_map/ppermute | solution.py:165
  258.5 0.8 copy-start.6
  260.2 15.8 %collective-permute-start.9 = (f32[1025,128]{1,0:T(8,128)}, f32[1025,128]{1,0:T(8,128)}, u32[]{:S(2)}, u32[]{:S(2)}) collective-permute-start(f32[1025,128]{1,0:T(8,128)} %pad_maximum_fusion.6), channel_id=1, source_target_pairs={{0,8},{4,12},{8,16},{12,20},{16,24},{20,28},{1,9},{5,13},{9,17},{1... | collective-permute-start | bytes 1574408 | tf_op jit(solution)/shard_map/ppermute | solution.py:165
  261.6 15.0 %copy-start.7 = (f32[1024,128]{1,0:T(8,128)S(1)}, f32[1024,128]{1,0:T(8,128)}, u32[]{:S(2)}) copy-start(f32[1024,128]{1,0:T(8,128)} %copy-done.6) | copy-start | bytes 1572868
  267.1 92.4 %collective-permute-start.8 = (f32[4,2,12,64,128]{4,3,2,1,0:T(8,128)}, f32[4,2,12,64,128]{4,3,2,1,0:T(8,128)}, u32[]{:S(2)}, u32[]{:S(2)}) collective-permute-start(f32[4,2,12,64,128]{4,3,2,1,0:T(8,128)} %get-tuple-element.31), channel_id=1, source_target_pairs={{0,1},{1,0},{2,3},{3,2},{4,5},{5,4},{6,7},{7,6},{8,9},{9,8},{10,11... | collective-permute-start | bytes 9437192 | tf_op jit(solution)/shard_map/ppermute | solution.py:198
  278.7 26.1 %collective-permute-start.10 = (f32[1025,128]{1,0:T(8,128)}, f32[1025,128]{1,0:T(8,128)}, u32[]{:S(2)}, u32[]{:S(2)}) collective-permute-start(f32[1025,128]{1,0:T(8,128)} %pad_maximum_fusion.7), channel_id=1, source_target_pairs={{0,16},{4,20},{8,24},{12,28},{1,17},{5,21},{9,25},{13,29},{2,18},{... | collective-permute-start | bytes 1574408 | tf_op jit(solution)/shard_map/ppermute | solution.py:165
  307.9 2.0 collective-permute-start.11
  314.1 45.5 %collective-permute-start.12 = (f32[4,2,4,64,128]{4,3,2,1,0:T(8,128)}, f32[4,2,4,64,128]{4,3,2,1,0:T(8,128)}, u32[]{:S(2)}, u32[]{:S(2)}) collective-permute-start(f32[4,2,4,64,128]{4,3,2,1,0:T(8,128)} %get-tuple-element.35), channel_id=1, source_target_pairs={{0,1},{1,0},{2,3},{3,2},{4,5},{5,4},{6,7},{7,6},{8,9},{9,8},{10,11... | collective-permute-start | bytes 3145736 | tf_op jit(solution)/shard_map/ppermute | solution.py:198
